TPU v7x, 32 devices: a whole 2x2x4 slice. The times are simulated.
32 devices in a mesh: grp: 4 (over z), emb: 8 (over y, x, core).
Axes of the slice: x: 2, y: 2, z: 4, core: 2. Of those that a mesh axis runs over, the one named last changes fastest.
Arguments:
- bottom_out: bfloat16 [4096, 128], P(('grp', 'emb')), may hold values from -6 to 6
- owner_ids: int32 [106496, 1], P(('grp', 'emb')), may hold values from 0 to 7; in each aligned block of 3328 rows (0 to 3327, 3328 to 6655, ...) at most 624 rows name the same one
- row_ids: int32 [4096, 26], P(('grp', 'emb')), may hold values from 0 to 95
- positions: int32 [4096], P(('grp', 'emb')), may hold values from 0 to 15
- labels: int32 [4096], P(('grp', 'emb')), may hold values 0 or 1
- tables: bfloat16 [26, 768, 128], P(None, 'emb'), may hold values from -6 to 6
- cross_down: bfloat16 [3456, 512], replicated, may hold values from -0.109375 to 0.109375
- cross_up: bfloat16 [512, 3456], replicated, may hold values from -0.25 to 0.25
- cross_bias: float32 [3456], replicated, may hold values from -3 to 3
- out_weight: bfloat16 [3456], replicated, may hold values from -0.109375 to 0.109375
- position_bias: float32 [16], replicated, may hold values from -2 to 2
Outputs:
- table_grad: float32 [26, 768, 128], P(None, 'emb')
- bottom_grad: bfloat16 [4096, 128], P(('grp', 'emb'))
- bias_grad: float32 [3456], replicated
Inputs may be any that keep to these rules, and one draw needn't show every extreme that they name: `owner_ids`: in every aligned block of 3328 lookups (the lookups of one device) no owner is named more than 624 times, and in some block one owner is named exactly 624 times.
All inputs are finite; a program needn't handle non-finite values. No bound on the sum of `labels` on one device may be relied on, other than what follows from the above.
Results may differ from a plain program's by a relative error of at most 0.0085.
Values may be sent and summed in bfloat16 or wider, within the bound.
No kernel may reach another device: no remote copies, remote signals or barrier semaphores. Data moves between devices by JAX's collectives and lax.ppermute only.
A program may use at most 64 MiB of HBM per device.

v0:
```python
import jax
import jax.numpy as jnp
from jax import lax
from jax.sharding import PartitionSpec as P


def local(
    bottom_out,
    owner_ids,
    row_ids,
    positions,
    labels,
    tables,
    cross_down,
    cross_up,
    cross_bias,
    out_weight,
    position_bias,
):
    sample_count, table_count = row_ids.shape
    rows_local = tables.shape[1]
    row_width = tables.shape[2]
    owner_count = lax.axis_size("emb")
    capacity = 3 * sample_count * table_count // (2 * owner_count)
    lookup_count = sample_count * table_count
    owners = owner_ids.reshape(sample_count, table_count)
    flat_owner = owners.reshape(-1)
    local_grid = jnp.arange(table_count, dtype=jnp.int32)[None, :] * rows_local + row_ids
    local_index = local_grid.reshape(-1)
    owner_marks = (flat_owner[:, None] == jnp.arange(owner_count, dtype=jnp.int32)[None, :]).astype(
        jnp.int32
    )
    ranking = jnp.cumsum(owner_marks, axis=0) - 1
    slot_index = jnp.sum(ranking * owner_marks, axis=1)
    buffer_place = flat_owner * capacity + slot_index
    flat_table = tables.reshape(table_count * rows_local, row_width)
    request = jnp.zeros((owner_count * capacity,), jnp.int32).at[buffer_place].set(local_index)
    request = request.reshape(owner_count, capacity)
    received = lax.all_to_all(request, "emb", split_axis=0, concat_axis=0, tiled=True)
    fetched = flat_table[received]
    arrived = lax.all_to_all(fetched, "emb", split_axis=0, concat_axis=0, tiled=True)
    pooled = arrived.reshape(owner_count * capacity, row_width)[buffer_place].reshape(
        sample_count, table_count * row_width
    )
    first = jnp.concatenate([bottom_out, pooled], axis=1)
    first_wide = first.astype(jnp.float32)
    weight_row = out_weight.astype(jnp.float32)
    reduced = jnp.dot(first, cross_down, preferred_element_type=jnp.float32).astype(jnp.bfloat16)
    gate_scale = jnp.dot(reduced, cross_up, preferred_element_type=jnp.float32) + cross_bias
    crossed = first_wide * gate_scale + first_wide
    position_marks = (
        positions[:, None] == jnp.arange(position_bias.shape[0], dtype=jnp.int32)[None, :]
    ).astype(jnp.float32)
    logit = jnp.sum(crossed * weight_row[None, :], axis=1) + jnp.sum(
        position_marks * position_bias[None, :], axis=1
    )
    err = jax.nn.sigmoid(logit) - labels.astype(jnp.float32)
    cotangent = err[:, None] * weight_row[None, :]
    scaled = cotangent * first_wide
    down_grad = lax.dot_general(
        scaled.astype(jnp.bfloat16),
        cross_up,
        (((1,), (1,)), ((), ())),
        preferred_element_type=jnp.float32,
    ).astype(jnp.bfloat16)
    back_term = lax.dot_general(
        down_grad, cross_down, (((1,), (1,)), ((), ())), preferred_element_type=jnp.float32
    )
    input_grad = (cotangent * (gate_scale + 1.0) + back_term).astype(jnp.bfloat16)
    bottom_grad = input_grad[:, :row_width]
    row_grads = input_grad[:, row_width:].reshape(lookup_count, row_width)
    outgoing = (
        jnp.zeros((owner_count * capacity, row_width), jnp.bfloat16).at[buffer_place].set(row_grads)
    )
    incoming = lax.all_to_all(
        outgoing.reshape(owner_count, capacity, row_width),
        "emb",
        split_axis=0,
        concat_axis=0,
        tiled=True,
    )
    local_grad = (
        jnp.zeros((table_count * rows_local, row_width), jnp.float32)
        .at[received.reshape(-1)]
        .add(incoming.reshape(owner_count * capacity, row_width).astype(jnp.float32))
    )
    summed_grad = lax.psum(local_grad.astype(jnp.bfloat16), "grp").astype(jnp.float32)
    table_grad = summed_grad.reshape(table_count, rows_local, row_width)
    bias_local = jnp.sum(scaled, axis=0)
    bias_grad = lax.psum(bias_local, ("grp", "emb"))
    return (table_grad, bottom_grad, bias_grad)


def solution(mesh):
    placed = (
        P(("grp", "emb"), None),
        P(("grp", "emb"), None),
        P(("grp", "emb"), None),
        P(("grp", "emb")),
        P(("grp", "emb")),
        P(None, "emb", None),
        P(),
        P(),
        P(),
        P(),
        P(),
    )
    return jax.shard_map(
        local,
        mesh=mesh,
        in_specs=placed,
        out_specs=(P(None, "emb", None), P(("grp", "emb"), None), P()),
        check_vma=False,
    )
```

profile of v0, /device:TPU:0, one launch (start us, length us, event | category | flops | bytes accessed | tf_op | source)
XLA Modules:
  0.0 242.6 jit_solution(920060485825970964)
XLA Ops:
  8.9 1.6 reshape.157
  11.9 5.2 %reduce-window.6 = s32[8,26,128]{2,1,0:T(8,128)} reduce-window(s32[8,26,128]{2,1,0:T(8,128)} %fusion.17, s32[]{:T(128)} %constant.10.clone.1), window={size=1x1x128 pad=0_0x0_0x127_0}, to_apply=%region_0.0 | reduce-window | flops 3381248 | bytes 212996 | tf_op jit(solution)/shard_map/reduce-window
  17.1 1.8 slice_reduce_fusion
  18.9 1.5 reduce-window.9
  22.2 13.5 %scatter_custom_fusion = s32[4992]{0:T(1024)} fusion(s32[3328]{0:T(1024)S(1)} %fusion.22, s32[3328]{0:T(1024)} %reshape.157, s32[]{:T(128)} %constant.10.clone.1), kind=kCustom, calls=%fused_computation.40 | custom fusion | bytes 20480 | tf_op jit(solution)/shard_map/scatter | solution.py:37
  37.1 9.9 %all_to_all.22 = s32[8,1,624]{2,1,0:T(1,128)S(1)} all-to-all(s32[8,1,624]{2,1,0:T(1,128)} %all_to_all.14), channel_id=1, replica_groups=mesh['grp'=4,'emb'=8] {'emb'}, dimensions={0} | all-to-all | bytes 39936 | tf_op jit(solution)/shard_map/all_to_all | solution.py:39
  51.1 12.3 %gather_fusion = bf16[4992,128]{1,0:T(8,128)(2,1)} fusion(bf16[2496,128]{1,0:T(8,128)(2,1)} %bitcast.32, s32[5120]{0:T(1024)} %pad_clamp_fusion), kind=kCustom, calls=%fused_computation | custom fusion | bytes 2575872 | tf_op jit(solution)/shard_map/gather | solution.py:40
  63.4 4.3 %all-to-all-start.1 = ((bf16[8,624,128]{2,1,0:T(8,128)(2,1)}), bf16[8,624,128]{2,1,0:T(8,128)(2,1)}, u32[]{:S(2)}, u32[]{:S(2)}) async-start(bf16[8,624,128]{2,1,0:T(8,128)(2,1)} %bitcast.34), calls=%async_computation.1 | async-start | bytes 2555904 | tf_op jit(solution)/shard_map/all_to_all | solution.py:41
  72.3 13.2 %all-to-all-done.1 = bf16[8,624,128]{2,1,0:T(8,128)(2,1)} async-done(((bf16[8,624,128]{2,1,0:T(8,128)(2,1)}), bf16[8,624,128]{2,1,0:T(8,128)(2,1)}, u32[]{:S(2)}, u32[]{:S(2)}) %all-to-all-start.1) | async-done | bytes 1277984 | tf_op jit(solution)/shard_map/all_to_all | solution.py:41
  85.5 9.2 %gather_fusion.1 = bf16[3328,128]{1,0:T(8,128)(2,1)} fusion(bf16[4992,128]{1,0:T(8,128)(2,1)} %bitcast.4, s32[4096]{0:T(1024)} %pad_clamp_fusion.1), kind=kCustom, calls=%fused_computation.1 | custom fusion | bytes 1717248 | tf_op jit(solution)/shard_map/gather | solution.py:42
  94.7 2.8 %reshape.131 = bf16[128,3328]{1,0:T(8,128)(2,1)} reshape(bf16[3328,128]{1,0:T(8,128)(2,1)} %gather_fusion.1) | data formatting | bytes 1703936 | tf_op jit(solution)/shard_map/reshape | solution.py:42
  97.5 2.1 constant_dynamic-update-slice_fusion
  99.6 5.6 %fusion.6 = (f32[128]{0:T(128)}, f32[128,3456]{1,0:T(8,128)}) fusion(bf16[128,3456]{1,0:T(8,128)(2,1)} %constant_dynamic-update-slice_fusion, f32[3456]{0:T(1024)S(1)} %convert_element_type.40, f32[3456]{0:T(1024)} %param.19, bf16[512,3456]{1,0:T(8,128)(2,1)} %param.18, bf16[3456,512]{1,0:T(8,128)(2,1)S(1)} %copy-done), kind=kOutput, calls=%fused_computation.16 | convolution fusion | flops 908689280 | bytes 9760256 | tf_op jit(solution)/shard_map/dot_general | solution.py:49
  106.4 6.1 %fusion = bf16[128,3456]{1,0:T(8,128)(2,1)} fusion(bf16[3456,512]{1,0:T(8,128)(2,1)S(1)} %copy-done, f32[128,3456]{1,0:T(8,128)} %get-tuple-element.4, bf16[512,3456]{1,0:T(8,128)(2,1)} %param.18, bf16[128,3456]{1,0:T(8,128)(2,1)} %constant_dynamic-update-slice_fusion, f32[128]{0:T(128)} %divide_subtract_fusion, f32[3456]{0:T(1024)S(1)} %convert_element_type.40), kind=kOutput, calls=%fused_computation.7 | convolution fusion | flops 910016512 | bytes 10631168 | tf_op jit(solution)/shard_map/dot_general | solution.py:66
  112.4 2.1 slice.21
  114.5 2.9 %reshape.165 = bf16[3328,128]{1,0:T(8,128)(2,1)} reshape(bf16[128,3328]{1,0:T(8,128)(2,1)} %slice.21) | data formatting | bytes 1703936 | tf_op jit(solution)/shard_map/reshape | solution.py:71
  117.4 14.9 %scatter_custom_fusion.1 = bf16[4992,128]{1,0:T(8,128)(2,1)} fusion(s32[3328]{0:T(1024)} %copy-done.2, bf16[3328,128]{1,0:T(8,128)(2,1)} %reshape.165, bf16[]{:T(256)} %constant.5.clone.1), kind=kCustom, calls=%fused_computation.21 | custom fusion | bytes 1278464 | tf_op jit(solution)/shard_map/scatter | solution.py:73
  132.3 4.3 %all-to-all-start.2 = ((bf16[8,624,128]{2,1,0:T(8,128)(2,1)}), bf16[8,624,128]{2,1,0:T(8,128)(2,1)}, u32[]{:S(2)}, u32[]{:S(2)}) async-start(bf16[8,624,128]{2,1,0:T(8,128)(2,1)} %bitcast.33), calls=%async_computation.2 | async-start | bytes 2555904 | tf_op jit(solution)/shard_map/all_to_all | solution.py:75
  141.0 13.4 %all-to-all-done.2 = bf16[8,624,128]{2,1,0:T(8,128)(2,1)} async-done(((bf16[8,624,128]{2,1,0:T(8,128)(2,1)}), bf16[8,624,128]{2,1,0:T(8,128)(2,1)}, u32[]{:S(2)}, u32[]{:S(2)}) %all-to-all-start.2) | async-done | bytes 1277984 | tf_op jit(solution)/shard_map/all_to_all | solution.py:75
  154.4 33.9 %scatter_custom_fusion.2 = f32[2496,128]{1,0:T(8,128)} fusion(s32[4992]{0:T(1024)} %fusion.21, bf16[4992,128]{1,0:T(8,128)(2,1)} %bitcast.8, f32[]{:T(128)} %constant.9.clone.1), kind=kCustom, calls=%fused_computation.9 | custom fusion | flops 1277952 | bytes 2556416 | tf_op jit(solution)/shard_map/scatter-add | solution.py:85
  188.4 2.2 convert_element_type.47
  192.0 2.1 fusion.3
  194.1 39.5 %psum.15 = f32[3456]{0:T(1024)} all-reduce(f32[3456]{0:T(1024)} %fusion.3), channel_id=1, replica_groups=mesh['grp'=4,'emb'=8] {'grp','emb'}, use_global_device_ids=true, to_apply=%region_10.11 | all-reduce | flops 3456 | bytes 27648 | tf_op jit(solution)/shard_map/psum | solution.py:90
  233.5 2.3 reshape.135
  (30 shorter events, 22.1 us)
Async XLA Ops:
  7.2 92.5 %copy-start = (bf16[3456,512]{1,0:T(8,128)(2,1)S(1)}, bf16[3456,512]{1,0:T(8,128)(2,1)}, u32[]{:S(2)}) copy-start(bf16[3456,512]{1,0:T(8,128)(2,1)} %param.17) | copy-start | bytes 10616836
  22.2 41.2 %copy-start.2 = (s32[3328]{0:T(1024)}, s32[3328]{0:T(1024)S(1)}, u32[]{:S(2)}) copy-start(s32[3328]{0:T(1024)S(1)} %fusion.22) | copy-start | bytes 39940
  47.1 0.6 copy-start.1
  63.4 22.1 %all-to-all-start.1 = ((bf16[8,624,128]{2,1,0:T(8,128)(2,1)}), bf16[8,624,128]{2,1,0:T(8,128)(2,1)}, u32[]{:S(2)}, u32[]{:S(2)}) async-start(bf16[8,624,128]{2,1,0:T(8,128)(2,1)} %bitcast.34), calls=%async_computation.1 | async-start | bytes 2555904 | tf_op jit(solution)/shard_map/all_to_all | solution.py:41
  132.3 22.1 %all-to-all-start.2 = ((bf16[8,624,128]{2,1,0:T(8,128)(2,1)}), bf16[8,624,128]{2,1,0:T(8,128)(2,1)}, u32[]{:S(2)}, u32[]{:S(2)}) async-start(bf16[8,624,128]{2,1,0:T(8,128)(2,1)} %bitcast.33), calls=%async_computation.2 | async-start | bytes 2555904 | tf_op jit(solution)/shard_map/all_to_all | solution.py:75
  136.5 97.0 %all-reduce.2.cloned.1.call-start = ((), (), s32[]{:S(2)}) async-start(), calls=%async_computation.3 | async-start | bytes 1277952 | tf_op jit(solution)/shard_map/psum | solution.py:87
Sparse Core Ops, SparseCore 0:
  190.7 39.9 all-reduce.1
where the time goes:
time: 245 us; the launch traced here: 243 us
  local copies, waits for them, and re-layouts  71.5 us (29%)
  other arithmetic  60.6 us (25%)
  blocking collectives  49.4 us (20%)
  waiting for transfers between devices  26.7 us (11%)
  between operations  14.1 us (6%)
  matrix products  11.6 us (5%)
  starting transfers between devices  8.73 us (4%)
    psum x1, blocking collectives, local(): bias_grad = lax.psum(bias_local, ('grp', 'emb'))  39.5 us
    scatter-add x1, other arithmetic, local(): local_grad = jnp.zeros((table_count * rows_local, row_width), jnp.float32...  33.9 us
    scatter x1, local copies, waits for them, and re-layouts, local(): jnp.zeros((owner_count * capacity, row_width), jnp.bfloat16)  14.9 us
    scatter x1, local copies, waits for them, and re-layouts, local(): jnp.zeros((owner_count * capacity,), jnp.int32).at[buffer_place]  13.5 us
    all_to_all x1, waiting for transfers between devices, local(): lax.all_to_all(outgoing.reshape(owner_count, capacity, row_width), 'emb',...  13.4 us
    all_to_all x1, waiting for transfers between devices, local(): lax.all_to_all(fetched, 'emb', split_axis=0, concat_axis=0, tiled=True)  13.2 us
    gather x1, local copies, waits for them, and re-layouts, local(): fetched = flat_table[received]  12.3 us
    all_to_all x1, blocking collectives, local(): lax.all_to_all(request, 'emb', split_axis=0, concat_axis=0, tiled=True)  9.94 us
  transfers between devices with their start and end apart: 3, of which 2 were waited for; matrix products, arithmetic and copies ran while one was open for 5% of the time, Pallas kernels for 0%

commit v1 on v0

--- a/solution.py
+++ b/solution.py
@@ -87,7 +87,7 @@
     summed_grad = lax.psum(local_grad.astype(jnp.bfloat16), "grp").astype(jnp.float32)
     table_grad = summed_grad.reshape(table_count, rows_local, row_width)
     bias_local = jnp.sum(scaled, axis=0)
-    bias_grad = lax.psum(bias_local, ("grp", "emb"))
+    bias_grad = lax.psum(lax.psum(bias_local, "emb"), "grp")
     return (table_grad, bottom_grad, bias_grad)
 
 

time: 245 us -> 248 us (1.012)
  blocking collectives: 49.4 us -> 52.5 us
    psum x1 -> x2, blocking collectives: 39.5 us -> 42.5 us  [local(): bias_grad = lax.psum(lax.psum(bias_local, 'emb'), 'grp')]
where the time goes in v1:
time: 248 us; the launch traced here: 246 us
  local copies, waits for them, and re-layouts  71.5 us (29%)
  other arithmetic  60.6 us (24%)
  blocking collectives  52.5 us (21%)
  waiting for transfers between devices  26.7 us (11%)
  between operations  14.1 us (6%)
  matrix products  11.6 us (5%)
  starting transfers between devices  8.73 us (4%)
    psum x2, blocking collectives, local(): bias_grad = lax.psum(lax.psum(bias_local, 'emb'), 'grp')  42.5 us
    scatter-add x1, other arithmetic, local(): local_grad = jnp.zeros((table_count * rows_local, row_width), jnp.float32...  33.9 us
    scatter x1, local copies, waits for them, and re-layouts, local(): jnp.zeros((owner_count * capacity, row_width), jnp.bfloat16)  14.9 us
    scatter x1, local copies, waits for them, and re-layouts, local(): jnp.zeros((owner_count * capacity,), jnp.int32).at[buffer_place]  13.5 us
    all_to_all x1, waiting for transfers between devices, local(): lax.all_to_all(outgoing.reshape(owner_count, capacity, row_width), 'emb',...  13.4 us
    all_to_all x1, waiting for transfers between devices, local(): lax.all_to_all(fetched, 'emb', split_axis=0, concat_axis=0, tiled=True)  13.2 us
    gather x1, local copies, waits for them, and re-layouts, local(): fetched = flat_table[received]  12.3 us
    all_to_all x1, blocking collectives, local(): lax.all_to_all(request, 'emb', split_axis=0, concat_axis=0, tiled=True)  9.94 us
  transfers between devices with their start and end apart: 3, of which 2 were waited for; matrix products, arithmetic and copies ran while one was open for 5% of the time, Pallas kernels for 0%

profile of v1, /device:TPU:0, one launch (start us, length us, event | category | flops | bytes accessed | tf_op | source)
XLA Modules:
  0.0 245.7 jit_solution(15678349157538925956)
XLA Ops:
  8.9 1.6 reshape.157
  11.9 5.2 %reduce-window.6 = s32[8,26,128]{2,1,0:T(8,128)} reduce-window(s32[8,26,128]{2,1,0:T(8,128)} %fusion.17, s32[]{:T(128)} %constant.10.clone.1), window={size=1x1x128 pad=0_0x0_0x127_0}, to_apply=%region_0.0 | reduce-window | flops 3381248 | bytes 212996 | tf_op jit(solution)/shard_map/reduce-window
  17.1 1.8 slice_reduce_fusion
  22.2 13.5 %scatter_custom_fusion = s32[4992]{0:T(1024)} fusion(s32[3328]{0:T(1024)S(1)} %fusion.22, s32[3328]{0:T(1024)} %reshape.157, s32[]{:T(128)} %constant.10.clone.1), kind=kCustom, calls=%fused_computation.40 | custom fusion | bytes 20480 | tf_op jit(solution)/shard_map/scatter | solution.py:37
  37.1 9.9 %all_to_all.22 = s32[8,1,624]{2,1,0:T(1,128)S(1)} all-to-all(s32[8,1,624]{2,1,0:T(1,128)} %all_to_all.14), channel_id=1, replica_groups=mesh['grp'=4,'emb'=8] {'emb'}, dimensions={0} | all-to-all | bytes 39936 | tf_op jit(solution)/shard_map/all_to_all | solution.py:39
  51.1 12.3 %gather_fusion = bf16[4992,128]{1,0:T(8,128)(2,1)} fusion(bf16[2496,128]{1,0:T(8,128)(2,1)} %bitcast.32, s32[5120]{0:T(1024)} %pad_clamp_fusion), kind=kCustom, calls=%fused_computation | custom fusion | bytes 2575872 | tf_op jit(solution)/shard_map/gather | solution.py:40
  63.4 4.3 %all-to-all-start.1 = ((bf16[8,624,128]{2,1,0:T(8,128)(2,1)}), bf16[8,624,128]{2,1,0:T(8,128)(2,1)}, u32[]{:S(2)}, u32[]{:S(2)}) async-start(bf16[8,624,128]{2,1,0:T(8,128)(2,1)} %bitcast.34), calls=%async_computation.1 | async-start | bytes 2555904 | tf_op jit(solution)/shard_map/all_to_all | solution.py:41
  72.3 13.2 %all-to-all-done.1 = bf16[8,624,128]{2,1,0:T(8,128)(2,1)} async-done(((bf16[8,624,128]{2,1,0:T(8,128)(2,1)}), bf16[8,624,128]{2,1,0:T(8,128)(2,1)}, u32[]{:S(2)}, u32[]{:S(2)}) %all-to-all-start.1) | async-done | bytes 1277984 | tf_op jit(solution)/shard_map/all_to_all | solution.py:41
  85.5 9.2 %gather_fusion.1 = bf16[3328,128]{1,0:T(8,128)(2,1)} fusion(bf16[4992,128]{1,0:T(8,128)(2,1)} %bitcast.4, s32[4096]{0:T(1024)} %pad_clamp_fusion.1), kind=kCustom, calls=%fused_computation.1 | custom fusion | bytes 1717248 | tf_op jit(solution)/shard_map/gather | solution.py:42
  94.7 2.8 %reshape.131 = bf16[128,3328]{1,0:T(8,128)(2,1)} reshape(bf16[3328,128]{1,0:T(8,128)(2,1)} %gather_fusion.1) | data formatting | bytes 1703936 | tf_op jit(solution)/shard_map/reshape | solution.py:42
  97.5 2.1 constant_dynamic-update-slice_fusion
  99.6 5.6 %fusion.6 = (f32[128]{0:T(128)}, f32[128,3456]{1,0:T(8,128)}) fusion(bf16[128,3456]{1,0:T(8,128)(2,1)} %constant_dynamic-update-slice_fusion, f32[3456]{0:T(1024)S(1)} %convert_element_type.40, f32[3456]{0:T(1024)} %param.19, bf16[512,3456]{1,0:T(8,128)(2,1)} %param.18, bf16[3456,512]{1,0:T(8,128)(2,1)S(1)} %copy-done), kind=kOutput, calls=%fused_computation.16 | convolution fusion | flops 908689280 | bytes 9760256 | tf_op jit(solution)/shard_map/dot_general | solution.py:49
  106.4 6.1 %fusion = bf16[128,3456]{1,0:T(8,128)(2,1)} fusion(bf16[3456,512]{1,0:T(8,128)(2,1)S(1)} %copy-done, f32[128,3456]{1,0:T(8,128)} %get-tuple-element.4, bf16[512,3456]{1,0:T(8,128)(2,1)} %param.18, bf16[128,3456]{1,0:T(8,128)(2,1)} %constant_dynamic-update-slice_fusion, f32[128]{0:T(128)} %divide_subtract_fusion, f32[3456]{0:T(1024)S(1)} %convert_element_type.40), kind=kOutput, calls=%fused_computation.7 | convolution fusion | flops 910016512 | bytes 10631168 | tf_op jit(solution)/shard_map/dot_general | solution.py:66
  112.4 2.1 slice.21
  114.5 2.9 %reshape.165 = bf16[3328,128]{1,0:T(8,128)(2,1)} reshape(bf16[128,3328]{1,0:T(8,128)(2,1)} %slice.21) | data formatting | bytes 1703936 | tf_op jit(solution)/shard_map/reshape | solution.py:71
  117.4 14.9 %scatter_custom_fusion.1 = bf16[4992,128]{1,0:T(8,128)(2,1)} fusion(s32[3328]{0:T(1024)} %copy-done.2, bf16[3328,128]{1,0:T(8,128)(2,1)} %reshape.165, bf16[]{:T(256)} %constant.5.clone.1), kind=kCustom, calls=%fused_computation.21 | custom fusion | bytes 1278464 | tf_op jit(solution)/shard_map/scatter | solution.py:73
  132.3 4.3 %all-to-all-start.2 = ((bf16[8,624,128]{2,1,0:T(8,128)(2,1)}), bf16[8,624,128]{2,1,0:T(8,128)(2,1)}, u32[]{:S(2)}, u32[]{:S(2)}) async-start(bf16[8,624,128]{2,1,0:T(8,128)(2,1)} %bitcast.33), calls=%async_computation.2 | async-start | bytes 2555904 | tf_op jit(solution)/shard_map/all_to_all | solution.py:75
  141.0 13.4 %all-to-all-done.2 = bf16[8,624,128]{2,1,0:T(8,128)(2,1)} async-done(((bf16[8,624,128]{2,1,0:T(8,128)(2,1)}), bf16[8,624,128]{2,1,0:T(8,128)(2,1)}, u32[]{:S(2)}, u32[]{:S(2)}) %all-to-all-start.2) | async-done | bytes 1277984 | tf_op jit(solution)/shard_map/all_to_all | solution.py:75
  154.4 33.9 %scatter_custom_fusion.2 = f32[2496,128]{1,0:T(8,128)} fusion(s32[4992]{0:T(1024)} %fusion.21, bf16[4992,128]{1,0:T(8,128)(2,1)} %bitcast.8, f32[]{:T(128)} %constant.9.clone.1), kind=kCustom, calls=%fused_computation.9 | custom fusion | flops 1277952 | bytes 2556416 | tf_op jit(solution)/shard_map/scatter-add | solution.py:85
  188.4 2.2 convert_element_type.47
  192.0 2.1 fusion.3
  194.1 23.6 %psum.22 = f32[3456]{0:T(1024)S(1)} all-reduce(f32[3456]{0:T(1024)} %fusion.3), channel_id=1, replica_groups=mesh['grp'=4,'emb'=8] {'emb'}, use_global_device_ids=true, to_apply=%region_10.11 | all-reduce | flops 3456 | bytes 27648 | tf_op jit(solution)/shard_map/psum | solution.py:90
  217.7 18.9 %psum.23 = f32[3456]{0:T(1024)} all-reduce(f32[3456]{0:T(1024)S(1)} %psum.22), channel_id=1, replica_groups=mesh['grp'=4,'emb'=8] {'grp'}, use_global_device_ids=true, to_apply=%region_11.12 | all-reduce | flops 3456 | bytes 27648 | tf_op jit(solution)/shard_map/psum | solution.py:90
  236.6 2.3 reshape.135
  (31 shorter events, 23.5 us)
Async XLA Ops:
  7.2 92.5 %copy-start = (bf16[3456,512]{1,0:T(8,128)(2,1)S(1)}, bf16[3456,512]{1,0:T(8,128)(2,1)}, u32[]{:S(2)}) copy-start(bf16[3456,512]{1,0:T(8,128)(2,1)} %param.17) | copy-start | bytes 10616836
  22.2 41.2 %copy-start.2 = (s32[3328]{0:T(1024)}, s32[3328]{0:T(1024)S(1)}, u32[]{:S(2)}) copy-start(s32[3328]{0:T(1024)S(1)} %fusion.22) | copy-start | bytes 39940
  47.1 0.6 copy-start.1
  63.4 22.1 %all-to-all-start.1 = ((bf16[8,624,128]{2,1,0:T(8,128)(2,1)}), bf16[8,624,128]{2,1,0:T(8,128)(2,1)}, u32[]{:S(2)}, u32[]{:S(2)}) async-start(bf16[8,624,128]{2,1,0:T(8,128)(2,1)} %bitcast.34), calls=%async_computation.1 | async-start | bytes 2555904 | tf_op jit(solution)/shard_map/all_to_all | solution.py:41
  132.3 22.1 %all-to-all-start.2 = ((bf16[8,624,128]{2,1,0:T(8,128)(2,1)}), bf16[8,624,128]{2,1,0:T(8,128)(2,1)}, u32[]{:S(2)}, u32[]{:S(2)}) async-start(bf16[8,624,128]{2,1,0:T(8,128)(2,1)} %bitcast.33), calls=%async_computation.2 | async-start | bytes 2555904 | tf_op jit(solution)/shard_map/all_to_all | solution.py:75
  136.5 100.1 %all-reduce.2.cloned.1.call-start = ((), (), s32[]{:S(2)}) async-start(), calls=%async_computation.3 | async-start | bytes 1277952 | tf_op jit(solution)/shard_map/psum | solution.py:87
Sparse Core Ops, SparseCore 0:
  190.7 40.0 all-reduce.1
